TPU v7x, 512 devices: a whole 4x8x8 slice. The times are simulated.
512 devices in a mesh: ind: 64 (over y, z), snp: 8 (over x, core).
Axes of the slice: x: 4, y: 8, z: 8, core: 2. Of those that a mesh axis runs over, the one named last changes fastest.
Arguments:
- genotypes: int32 [4096, 16384], P('ind', 'snp'), may hold values from 0 to 2
- observed: int32 [4096, 16384], P('ind', 'snp'), may hold values from 0 to 1
- ancestry: float32 [4096, 32], P('ind'), may hold values from 0.018 to 54.6, as said below
- freqs: float32 [16384, 32], P(('snp', 'ind')), may hold values from 0.05 to 0.95
Outputs:
- ancestry_out: float32 [4096, 32], P('ind')
- freqs_out: float32 [16384, 32], P(('snp', 'ind'))
Inputs may be any that keep to these rules, and one draw needn't show every extreme that they name: `ancestry`: positive weights.
All inputs are finite; a program needn't handle non-finite values.
Results may differ from a plain program's by a relative error of at most 0.0003.
Values sent between devices are 32-bit elements; how exact they have to be, the bound alone decides.
No kernel may reach another device: no remote copies, remote signals or barrier semaphores. Data moves between devices by JAX's collectives and lax.ppermute only.
A program may use at most 64 MiB of HBM per device.

v0:
```python
import jax
import jax.numpy as jnp
from jax import lax
from jax.sharding import PartitionSpec as P

STEPS = 3
clip_low = 1e-05
high = lax.Precision.HIGHEST


def over_rows(left, right):
    return lax.dot_general(
        left, right, (((0,), (0,)), ((), ())), precision=high, preferred_element_type=jnp.float32
    )


def per_device(genotypes, observed, ancestry, freqs):
    ind_count = lax.axis_size("ind")
    snp_count = lax.axis_size("snp")
    geno = genotypes.astype(jnp.float32)
    seen = observed.astype(jnp.float32)
    hits = seen * geno
    misses = seen * (2.0 - geno)
    own_rows = freqs.shape[0]
    q_zero = ancestry / jnp.sum(ancestry, axis=1, keepdims=True)
    f_zero = lax.all_gather(freqs, "ind", axis=0, tiled=True)
    f_weight = 1.0 / ind_count
    q_weight = 1.0 / snp_count

    def em_map(q_rows, f_state):
        prob = jnp.dot(q_rows, f_state.T, precision=high, preferred_element_type=jnp.float32)
        ratio_a = hits / prob
        ratio_b = misses / (1.0 - prob)
        sum_a = jnp.dot(ratio_a, f_state, precision=high, preferred_element_type=jnp.float32)
        sum_b = jnp.dot(ratio_b, 1.0 - f_state, precision=high, preferred_element_type=jnp.float32)
        c_part = over_rows(ratio_a, q_rows)
        d_part = over_rows(ratio_b, q_rows)
        sum_a, sum_b = lax.psum((sum_a, sum_b), "snp")
        q_next = q_rows * (sum_a + sum_b)
        q_next = q_next / jnp.sum(q_next, axis=1, keepdims=True)
        c_total, d_total = lax.psum((c_part, d_part), "ind")
        f_next = f_state * c_total / (f_state * c_total + (1.0 - f_state) * d_total)
        return (q_next, f_next)

    for step in range(STEPS):
        q_one, f_one = em_map(q_zero, f_zero)
        rq = q_one - q_zero
        rf = f_one - f_zero
        first_local = q_weight * jnp.sum(rq * rq) + f_weight * jnp.sum(rf * rf)
        q_two, f_two = em_map(q_one, f_one)
        vq = q_two - 2.0 * q_one + q_zero
        vf = f_two - 2.0 * f_one + f_zero
        second_local = q_weight * jnp.sum(vq * vq) + f_weight * jnp.sum(vf * vf)
        first, second = lax.psum((first_local, second_local), ("ind", "snp"))
        alpha = -jnp.sqrt(first / (second + 1e-20))
        q_ext = jnp.clip(q_zero - 2.0 * alpha * rq + alpha * alpha * vq, clip_low, 1.0 - clip_low)
        q_zero = q_ext / jnp.sum(q_ext, axis=1, keepdims=True)
        f_zero = jnp.clip(f_zero - 2.0 * alpha * rf + alpha * alpha * vf, clip_low, 1.0 - clip_low)
    f_final = lax.dynamic_slice_in_dim(f_zero, lax.axis_index("ind") * own_rows, own_rows, 0)
    return (q_zero, f_final)


def solution(mesh):
    in_specs = (P("ind", "snp"), P("ind", "snp"), P("ind", None), P(("snp", "ind"), None))
    out_specs = (P("ind", None), P(("snp", "ind"), None))
    return jax.shard_map(
        per_device, mesh=mesh, in_specs=in_specs, out_specs=out_specs, check_vma=False
    )
```

profile of v0, /device:TPU:1, one launch (start us, length us, event | category | flops | bytes accessed | tf_op | source)
XLA Modules:
  0.0 1308.1 jit_solution(10451656634871468365)
XLA Ops:
  7.2 47.0 %all_gather.3 = f32[2048,32]{1,0:T(8,128)S(1)} all-gather(f32[32,32]{1,0:T(8,128)} %param.7), channel_id=1, replica_groups=mesh['ind'=64,'snp'=8] {'ind'}, dimensions={0}, use_global_device_ids=true | all-gather | bytes 266240 | tf_op jit(solution)/shard_map/all_gather | solution.py:26
  54.3 1.3 fusion.48
  56.9 1.2 fusion.45
  59.1 1.8 convolution_add_fusion
  60.9 32.1 %psum.240 = f32[64,32]{0,1:T(8,128)S(1)} all-reduce(f32[64,32]{0,1:T(8,128)S(1)} %convolution_add_fusion), channel_id=1, replica_groups=mesh['ind'=64,'snp'=8] {'snp'}, use_global_device_ids=true, to_apply=%region_1.0 | all-reduce | flops 2048 | bytes 16384 | tf_op jit(solution)/shard_map/psum | solution.py:38
  93.0 123.9 %all-reduce.26.cloned.1.call-done = (f32[2048,32]{0,1:T(8,128)}, f32[2048,32]{0,1:T(8,128)}) async-done(((f32[2048,32]{0,1:T(8,128)}, f32[2048,32]{0,1:T(8,128)}), (f32[2048,32]{0,1:T(8,128)}, f32[2048,32]{0,1:T(8,128)})) %all-reduce.26.cloned.1.call-update) | async-done | bytes 524304 | tf_op jit(solution)/shard_map/psum | solution.py:41
  216.9 1.7 multiply_reduce_fusion.5
  219.2 1.2 fusion.27
  220.4 1.2 fusion.28
  222.9 24.9 %psum.241 = f32[64,32]{0,1:T(8,128)S(1)} all-reduce(f32[64,32]{0,1:T(8,128)S(1)} %convolution_add_fusion.5), channel_id=1, replica_groups=mesh['ind'=64,'snp'=8] {'snp'}, use_global_device_ids=true, to_apply=%region_9.0 | all-reduce | flops 2048 | bytes 16384 | tf_op jit(solution)/shard_map/psum | solution.py:38
  250.5 123.8 %all-reduce.24.cloned.1.call-done = (f32[2048,32]{0,1:T(8,128)}, f32[2048,32]{0,1:T(8,128)}) async-done(((f32[2048,32]{0,1:T(8,128)}, f32[2048,32]{0,1:T(8,128)}), (f32[2048,32]{0,1:T(8,128)}, f32[2048,32]{0,1:T(8,128)})) %all-reduce.24.cloned.1.call-update) | async-done | bytes 524304 | tf_op jit(solution)/shard_map/psum | solution.py:41
  374.3 1.7 multiply_reduce_fusion.4
  376.7 99.3 %all-reduce.2 = (f32[]{:T(128)}, f32[]{:T(128)}) all-reduce(f32[]{:T(128)S(6)} %add.164, f32[]{:T(128)S(6)} %add.169), channel_id=1, replica_groups=mesh['ind'=64,'snp'=8] {'ind','snp'}, use_global_device_ids=true, to_apply=%region_8.0 | all-reduce | flops 2 | bytes 16 | tf_op jit(solution)/shard_map/psum | solution.py:54
  478.1 1.2 fusion.49
  481.8 20.9 %psum.242 = f32[64,32]{0,1:T(8,128)S(1)} all-reduce(f32[64,32]{0,1:T(8,128)S(1)} %convolution_add_fusion.4), channel_id=1, replica_groups=mesh['ind'=64,'snp'=8] {'snp'}, use_global_device_ids=true, to_apply=%region_18.19 | all-reduce | flops 2048 | bytes 16384 | tf_op jit(solution)/shard_map/psum | solution.py:38
  502.7 125.4 %all-reduce.22.cloned.1.call-done = (f32[2048,32]{0,1:T(8,128)}, f32[2048,32]{0,1:T(8,128)}) async-done(((f32[2048,32]{0,1:T(8,128)}, f32[2048,32]{0,1:T(8,128)}), (f32[2048,32]{0,1:T(8,128)}, f32[2048,32]{0,1:T(8,128)})) %all-reduce.22.cloned.1.call-update) | async-done | bytes 524304 | tf_op jit(solution)/shard_map/psum | solution.py:41
  628.1 1.7 multiply_reduce_fusion.3
  630.4 1.2 fusion.33
  634.8 24.9 %psum.243 = f32[64,32]{0,1:T(8,128)S(1)} all-reduce(f32[64,32]{0,1:T(8,128)S(1)} %convolution_add_fusion.3), channel_id=1, replica_groups=mesh['ind'=64,'snp'=8] {'snp'}, use_global_device_ids=true, to_apply=%region_26.27 | all-reduce | flops 2048 | bytes 16384 | tf_op jit(solution)/shard_map/psum | solution.py:38
  661.6 123.9 %all-reduce.20.cloned.1.call-done = (f32[2048,32]{0,1:T(8,128)}, f32[2048,32]{0,1:T(8,128)}) async-done(((f32[2048,32]{0,1:T(8,128)}, f32[2048,32]{0,1:T(8,128)}), (f32[2048,32]{0,1:T(8,128)}, f32[2048,32]{0,1:T(8,128)})) %all-reduce.20.cloned.1.call-update) | async-done | bytes 524304 | tf_op jit(solution)/shard_map/psum | solution.py:41
  785.6 1.7 multiply_reduce_fusion.2
  787.9 99.4 %all-reduce.1 = (f32[]{:T(128)}, f32[]{:T(128)}) all-reduce(f32[]{:T(128)S(6)} %add.175, f32[]{:T(128)S(6)} %add.180), channel_id=1, replica_groups=mesh['ind'=64,'snp'=8] {'ind','snp'}, use_global_device_ids=true, to_apply=%region_25.26 | all-reduce | flops 2 | bytes 16 | tf_op jit(solution)/shard_map/psum | solution.py:54
  889.4 1.2 fusion.53
  893.1 20.8 %psum.244 = f32[64,32]{0,1:T(8,128)S(1)} all-reduce(f32[64,32]{0,1:T(8,128)S(1)} %convolution_add_fusion.2), channel_id=1, replica_groups=mesh['ind'=64,'snp'=8] {'snp'}, use_global_device_ids=true, to_apply=%region_35.36 | all-reduce | flops 2048 | bytes 16384 | tf_op jit(solution)/shard_map/psum | solution.py:38
  913.9 125.4 %all-reduce.18.cloned.1.call-done = (f32[2048,32]{0,1:T(8,128)}, f32[2048,32]{0,1:T(8,128)}) async-done(((f32[2048,32]{0,1:T(8,128)}, f32[2048,32]{0,1:T(8,128)}), (f32[2048,32]{0,1:T(8,128)}, f32[2048,32]{0,1:T(8,128)})) %all-reduce.18.cloned.1.call-update) | async-done | bytes 524304 | tf_op jit(solution)/shard_map/psum | solution.py:41
  1039.3 1.7 multiply_reduce_fusion.1
  1041.6 1.2 fusion.40
  1042.9 1.2 fusion.39
  1045.9 24.9 %psum.245 = f32[64,32]{0,1:T(8,128)S(1)} all-reduce(f32[64,32]{0,1:T(8,128)S(1)} %convolution_add_fusion.1), channel_id=1, replica_groups=mesh['ind'=64,'snp'=8] {'snp'}, use_global_device_ids=true, to_apply=%region_43.44 | all-reduce | flops 2048 | bytes 16384 | tf_op jit(solution)/shard_map/psum | solution.py:38
  1072.8 124.0 %all-reduce.16.cloned.1.call-done = (f32[2048,32]{0,1:T(8,128)}, f32[2048,32]{0,1:T(8,128)}) async-done(((f32[2048,32]{0,1:T(8,128)}, f32[2048,32]{0,1:T(8,128)}), (f32[2048,32]{0,1:T(8,128)}, f32[2048,32]{0,1:T(8,128)})) %all-reduce.16.cloned.1.call-update) | async-done | bytes 524304 | tf_op jit(solution)/shard_map/psum | solution.py:41
  1196.8 1.7 multiply_reduce_fusion
  1199.2 99.3 %all-reduce = (f32[]{:T(128)}, f32[]{:T(128)}) all-reduce(f32[]{:T(128)S(6)} %add.186, f32[]{:T(128)S(6)} %add.191), channel_id=1, replica_groups=mesh['ind'=64,'snp'=8] {'ind','snp'}, use_global_device_ids=true, to_apply=%region_42.43 | all-reduce | flops 2 | bytes 16 | tf_op jit(solution)/shard_map/psum | solution.py:54
  (58 shorter events, 18.9 us)
Async XLA Ops:
  7.2 47.0 %copy-start.2 = (f32[64,32]{0,1:T(8,128)S(1)}, f32[64,32]{0,1:T(8,128)}, u32[]{:S(2)}) copy-start(f32[64,32]{0,1:T(8,128)} %param.6) | copy-start | bytes 24580
  7.2 209.7 %all-reduce.26.cloned.1.call-start = ((), (), s32[]{:S(2)}) async-start(), calls=%async_computation.5 | async-start | bytes 1048576 | tf_op jit(solution)/shard_map/psum | solution.py:41
  54.2 1.3 copy-start
  54.2 1.3 copy-start.1
  58.2 316.1 %all-reduce.24.cloned.1.call-start = ((), (), s32[]{:S(2)}) async-start(), calls=%async_computation.4 | async-start | bytes 1048576 | tf_op jit(solution)/shard_map/psum | solution.py:41
  221.7 406.4 %all-reduce.22.cloned.1.call-start = ((), (), s32[]{:S(2)}) async-start(), calls=%async_computation.3 | async-start | bytes 1048576 | tf_op jit(solution)/shard_map/psum | solution.py:41
  480.6 305.0 %all-reduce.20.cloned.1.call-start = ((), (), s32[]{:S(2)}) async-start(), calls=%async_computation.2 | async-start | bytes 1048576 | tf_op jit(solution)/shard_map/psum | solution.py:41
  632.9 406.4 %all-reduce.18.cloned.1.call-start = ((), (), s32[]{:S(2)}) async-start(), calls=%async_computation.1 | async-start | bytes 1048576 | tf_op jit(solution)/shard_map/psum | solution.py:41
  891.8 304.9 %all-reduce.16.cloned.1.call-start = ((), (), s32[]{:S(2)}) async-start(), calls=%async_computation | async-start | bytes 1048576 | tf_op jit(solution)/shard_map/psum | solution.py:41
Sparse Core Ops, SparseCore 0:
  58.3 158.5 all-reduce.25
  221.8 152.4 all-reduce.23
  480.7 147.3 all-reduce.21
  633.0 152.4 all-reduce.19
  892.0 147.2 all-reduce.17
  1044.2 152.5 all-reduce.15
where the time goes:
time: 1310 us
  waiting for transfers between devices  746 us (57%)
  blocking collectives  494 us (38%)
  matrix products  27.2 us (2%)
  between operations  26.2 us (2%)
  other arithmetic  13.5 us (1%)
    psum x6, waiting for transfers between devices, em_map(): c_total, d_total = lax.psum((c_part, d_part), 'ind')  746 us
    psum x3, blocking collectives, per_device(): first, second = lax.psum((first_local, second_local), ('ind', 'snp'))  298 us
    psum x6, blocking collectives, em_map(): sum_a, sum_b = lax.psum((sum_a, sum_b), 'snp')  148 us
    all_gather x1, blocking collectives, per_device(): f_zero = lax.all_gather(freqs, 'ind', axis=0, tiled=True)  47 us
  transfers between devices with their start and end apart: 6, of which 6 were waited for; matrix products, arithmetic and copies ran while one was open for 1% of the time, Pallas kernels for 0%

commit v1 on v0

--- a/solution.py
+++ b/solution.py
@@ -51,7 +51,7 @@
         vq = q_two - 2.0 * q_one + q_zero
         vf = f_two - 2.0 * f_one + f_zero
         second_local = q_weight * jnp.sum(vq * vq) + f_weight * jnp.sum(vf * vf)
-        first, second = lax.psum((first_local, second_local), ("ind", "snp"))
+        first, second = lax.psum(lax.psum((first_local, second_local), "ind"), "snp")
         alpha = -jnp.sqrt(first / (second + 1e-20))
         q_ext = jnp.clip(q_zero - 2.0 * alpha * rq + alpha * alpha * vq, clip_low, 1.0 - clip_low)
         q_zero = q_ext / jnp.sum(q_ext, axis=1, keepdims=True)

time: 1310 us -> 1480 us (1.13)
  blocking collectives: 494 us -> 673 us
    psum x3 -> x6, blocking collectives: 298 us -> 477 us  [the longest x3 341 us: per_device(): lax.psum((first_local, second_local), 'ind')]
where the time goes in v1:
time: 1480 us
  waiting for transfers between devices  739 us (50%)
  blocking collectives  673 us (45%)
  matrix products  27.2 us (2%)
  between operations  26.2 us (2%)
    psum x6, waiting for transfers between devices, em_map(): c_total, d_total = lax.psum((c_part, d_part), 'ind')  739 us
    psum x3, blocking collectives, per_device(): lax.psum((first_local, second_local), 'ind')  341 us
    psum x6, blocking collectives, em_map(): sum_a, sum_b = lax.psum((sum_a, sum_b), 'snp')  149 us
    psum x3, blocking collectives, per_device(): lax.psum(lax.psum((first_local, second_local), 'ind'), 'snp')  136 us
    all_gather x1, blocking collectives, per_device(): f_zero = lax.all_gather(freqs, 'ind', axis=0, tiled=True)  47 us
  transfers between devices with their start and end apart: 6, of which 6 were waited for; matrix products, arithmetic and copies ran while one was open for 1% of the time, Pallas kernels for 0%

profile of v1, /device:TPU:1, one launch (start us, length us, event | category | flops | bytes accessed | tf_op | source)
XLA Modules:
  0.0 1479.9 jit_solution(11154453667311599493)
XLA Ops:
  7.2 47.0 %all_gather.3 = f32[2048,32]{1,0:T(8,128)S(1)} all-gather(f32[32,32]{1,0:T(8,128)} %param.7), channel_id=1, replica_groups=mesh['ind'=64,'snp'=8] {'ind'}, dimensions={0}, use_global_device_ids=true | all-gather | bytes 266240 | tf_op jit(solution)/shard_map/all_gather | solution.py:26
  54.3 1.3 fusion.48
  56.9 1.2 fusion.45
  59.1 1.8 convolution_add_fusion
  60.9 32.1 %psum.288 = f32[64,32]{0,1:T(8,128)S(1)} all-reduce(f32[64,32]{0,1:T(8,128)S(1)} %convolution_add_fusion), channel_id=1, replica_groups=mesh['ind'=64,'snp'=8] {'snp'}, use_global_device_ids=true, to_apply=%region_1.0 | all-reduce | flops 2048 | bytes 16384 | tf_op jit(solution)/shard_map/psum | solution.py:38
  93.0 123.9 %all-reduce.29.cloned.1.call-done = (f32[2048,32]{0,1:T(8,128)}, f32[2048,32]{0,1:T(8,128)}) async-done(((f32[2048,32]{0,1:T(8,128)}, f32[2048,32]{0,1:T(8,128)}), (f32[2048,32]{0,1:T(8,128)}, f32[2048,32]{0,1:T(8,128)})) %all-reduce.29.cloned.1.call-update) | async-done | bytes 524304 | tf_op jit(solution)/shard_map/psum | solution.py:41
  216.9 1.7 multiply_reduce_fusion.5
  219.2 1.2 fusion.27
  222.9 24.9 %psum.289 = f32[64,32]{0,1:T(8,128)S(1)} all-reduce(f32[64,32]{0,1:T(8,128)S(1)} %convolution_add_fusion.5), channel_id=1, replica_groups=mesh['ind'=64,'snp'=8] {'snp'}, use_global_device_ids=true, to_apply=%region_10.0 | all-reduce | flops 2048 | bytes 16384 | tf_op jit(solution)/shard_map/psum | solution.py:38
  250.5 123.8 %all-reduce.27.cloned.1.call-done = (f32[2048,32]{0,1:T(8,128)}, f32[2048,32]{0,1:T(8,128)}) async-done(((f32[2048,32]{0,1:T(8,128)}, f32[2048,32]{0,1:T(8,128)}), (f32[2048,32]{0,1:T(8,128)}, f32[2048,32]{0,1:T(8,128)})) %all-reduce.27.cloned.1.call-update) | async-done | bytes 524304 | tf_op jit(solution)/shard_map/psum | solution.py:41
  374.3 1.7 multiply_reduce_fusion.4
  376.7 113.6 %all-reduce.2 = (f32[]{:T(128)}, f32[]{:T(128)}) all-reduce(f32[]{:T(128)S(6)} %add.176, f32[]{:T(128)S(6)} %add.181), channel_id=1, replica_groups=mesh['ind'=64,'snp'=8] {'ind'}, use_global_device_ids=true, to_apply=%region_8.0 | all-reduce | flops 2 | bytes 16 | tf_op jit(solution)/shard_map/psum | solution.py:54
  490.3 45.3 %all-reduce.11 = (f32[]{:T(128)}, f32[]{:T(128)}) all-reduce(f32[]{:T(128)} %get-tuple-element.16, f32[]{:T(128)} %get-tuple-element.17), channel_id=1, replica_groups=mesh['ind'=64,'snp'=8] {'snp'}, use_global_device_ids=true, to_apply=%region_9.0 | all-reduce | flops 2 | bytes 16 | tf_op jit(solution)/shard_map/psum | solution.py:54
  537.6 1.2 fusion.49
  541.3 21.2 %psum.290 = f32[64,32]{0,1:T(8,128)S(1)} all-reduce(f32[64,32]{0,1:T(8,128)S(1)} %convolution_add_fusion.4), channel_id=1, replica_groups=mesh['ind'=64,'snp'=8] {'snp'}, use_global_device_ids=true, to_apply=%region_20.21 | all-reduce | flops 2048 | bytes 16384 | tf_op jit(solution)/shard_map/psum | solution.py:38
  562.6 121.6 %all-reduce.25.cloned.1.call-done = (f32[2048,32]{0,1:T(8,128)}, f32[2048,32]{0,1:T(8,128)}) async-done(((f32[2048,32]{0,1:T(8,128)}, f32[2048,32]{0,1:T(8,128)}), (f32[2048,32]{0,1:T(8,128)}, f32[2048,32]{0,1:T(8,128)})) %all-reduce.25.cloned.1.call-update) | async-done | bytes 524304 | tf_op jit(solution)/shard_map/psum | solution.py:41
  684.2 1.7 multiply_reduce_fusion.3
  686.5 1.2 fusion.33
  690.9 24.9 %psum.291 = f32[64,32]{0,1:T(8,128)S(1)} all-reduce(f32[64,32]{0,1:T(8,128)S(1)} %convolution_add_fusion.3), channel_id=1, replica_groups=mesh['ind'=64,'snp'=8] {'snp'}, use_global_device_ids=true, to_apply=%region_29.30 | all-reduce | flops 2048 | bytes 16384 | tf_op jit(solution)/shard_map/psum | solution.py:38
  717.7 123.9 %all-reduce.23.cloned.1.call-done = (f32[2048,32]{0,1:T(8,128)}, f32[2048,32]{0,1:T(8,128)}) async-done(((f32[2048,32]{0,1:T(8,128)}, f32[2048,32]{0,1:T(8,128)}), (f32[2048,32]{0,1:T(8,128)}, f32[2048,32]{0,1:T(8,128)})) %all-reduce.23.cloned.1.call-update) | async-done | bytes 524304 | tf_op jit(solution)/shard_map/psum | solution.py:41
  841.7 1.7 multiply_reduce_fusion.2
  844.1 113.6 %all-reduce.1 = (f32[]{:T(128)}, f32[]{:T(128)}) all-reduce(f32[]{:T(128)S(6)} %add.187, f32[]{:T(128)S(6)} %add.192), channel_id=1, replica_groups=mesh['ind'=64,'snp'=8] {'ind'}, use_global_device_ids=true, to_apply=%region_27.28 | all-reduce | flops 2 | bytes 16 | tf_op jit(solution)/shard_map/psum | solution.py:54
  957.6 45.3 %all-reduce.10 = (f32[]{:T(128)}, f32[]{:T(128)}) all-reduce(f32[]{:T(128)} %get-tuple-element.14, f32[]{:T(128)} %get-tuple-element.15), channel_id=1, replica_groups=mesh['ind'=64,'snp'=8] {'snp'}, use_global_device_ids=true, to_apply=%region_28.29 | all-reduce | flops 2 | bytes 16 | tf_op jit(solution)/shard_map/psum | solution.py:54
  1005.0 1.2 fusion.53
  1008.7 20.9 %psum.292 = f32[64,32]{0,1:T(8,128)S(1)} all-reduce(f32[64,32]{0,1:T(8,128)S(1)} %convolution_add_fusion.2), channel_id=1, replica_groups=mesh['ind'=64,'snp'=8] {'snp'}, use_global_device_ids=true, to_apply=%region_39.40 | all-reduce | flops 2048 | bytes 16384 | tf_op jit(solution)/shard_map/psum | solution.py:38
  1029.6 122.0 %all-reduce.21.cloned.1.call-done = (f32[2048,32]{0,1:T(8,128)}, f32[2048,32]{0,1:T(8,128)}) async-done(((f32[2048,32]{0,1:T(8,128)}, f32[2048,32]{0,1:T(8,128)}), (f32[2048,32]{0,1:T(8,128)}, f32[2048,32]{0,1:T(8,128)})) %all-reduce.21.cloned.1.call-update) | async-done | bytes 524304 | tf_op jit(solution)/shard_map/psum | solution.py:41
  1151.6 1.7 multiply_reduce_fusion.1
  1158.2 24.9 %psum.293 = f32[64,32]{0,1:T(8,128)S(1)} all-reduce(f32[64,32]{0,1:T(8,128)S(1)} %convolution_add_fusion.1), channel_id=1, replica_groups=mesh['ind'=64,'snp'=8] {'snp'}, use_global_device_ids=true, to_apply=%region_48.49 | all-reduce | flops 2048 | bytes 16384 | tf_op jit(solution)/shard_map/psum | solution.py:38
  1185.1 123.9 %all-reduce.19.cloned.1.call-done = (f32[2048,32]{0,1:T(8,128)}, f32[2048,32]{0,1:T(8,128)}) async-done(((f32[2048,32]{0,1:T(8,128)}, f32[2048,32]{0,1:T(8,128)}), (f32[2048,32]{0,1:T(8,128)}, f32[2048,32]{0,1:T(8,128)})) %all-reduce.19.cloned.1.call-update) | async-done | bytes 524304 | tf_op jit(solution)/shard_map/psum | solution.py:41
  1309.0 1.7 multiply_reduce_fusion
  1311.4 113.6 %all-reduce = (f32[]{:T(128)}, f32[]{:T(128)}) all-reduce(f32[]{:T(128)S(6)} %add.198, f32[]{:T(128)S(6)} %add.203), channel_id=1, replica_groups=mesh['ind'=64,'snp'=8] {'ind'}, use_global_device_ids=true, to_apply=%region_46.47 | all-reduce | flops 2 | bytes 16 | tf_op jit(solution)/shard_map/psum | solution.py:54
  1425.0 45.3 %all-reduce.9 = (f32[]{:T(128)}, f32[]{:T(128)}) all-reduce(f32[]{:T(128)} %get-tuple-element.12, f32[]{:T(128)} %get-tuple-element.13), channel_id=1, replica_groups=mesh['ind'=64,'snp'=8] {'snp'}, use_global_device_ids=true, to_apply=%region_47.48 | all-reduce | flops 2 | bytes 16 | tf_op jit(solution)/shard_map/psum | solution.py:54
  (61 shorter events, 22.5 us)
Async XLA Ops:
  7.2 47.0 %copy-start.2 = (f32[64,32]{0,1:T(8,128)S(1)}, f32[64,32]{0,1:T(8,128)}, u32[]{:S(2)}) copy-start(f32[64,32]{0,1:T(8,128)} %param.6) | copy-start | bytes 24580
  7.2 209.7 %all-reduce.29.cloned.1.call-start = ((), (), s32[]{:S(2)}) async-start(), calls=%async_computation.5 | async-start | bytes 1048576 | tf_op jit(solution)/shard_map/psum | solution.py:41
  54.2 1.3 copy-start
  54.2 1.3 copy-start.1
  58.2 316.1 %all-reduce.27.cloned.1.call-start = ((), (), s32[]{:S(2)}) async-start(), calls=%async_computation.4 | async-start | bytes 1048576 | tf_op jit(solution)/shard_map/psum | solution.py:41
  221.7 462.5 %all-reduce.25.cloned.1.call-start = ((), (), s32[]{:S(2)}) async-start(), calls=%async_computation.3 | async-start | bytes 1048576 | tf_op jit(solution)/shard_map/psum | solution.py:41
  540.1 301.6 %all-reduce.23.cloned.1.call-start = ((), (), s32[]{:S(2)}) async-start(), calls=%async_computation.2 | async-start | bytes 1048576 | tf_op jit(solution)/shard_map/psum | solution.py:41
  689.0 462.6 %all-reduce.21.cloned.1.call-start = ((), (), s32[]{:S(2)}) async-start(), calls=%async_computation.1 | async-start | bytes 1048576 | tf_op jit(solution)/shard_map/psum | solution.py:41
  1007.5 301.6 %all-reduce.19.cloned.1.call-start = ((), (), s32[]{:S(2)}) async-start(), calls=%async_computation | async-start | bytes 1048576 | tf_op jit(solution)/shard_map/psum | solution.py:41
Sparse Core Ops, SparseCore 0:
  58.3 158.5 all-reduce.28
  221.8 152.4 all-reduce.26
  540.2 143.9 all-reduce.24
  689.1 152.4 all-reduce.22
  1007.6 143.9 all-reduce.20
  1156.5 152.4 all-reduce.18
